TPU v7x, 32 devices: a whole 2x2x4 slice. The times are simulated.
32 devices in a mesh: chain: 8 (over z, x), grp: 4 (over y, core).
Axes of the slice: x: 2, y: 2, z: 4, core: 2. Of those that a mesh axis runs over, the one named last changes fastest.
Arguments:
- right_side: float32 [16, 4, 64, 128], P('chain', 'grp'), may hold values from -0.8 to 0.8
- factor: float32 [16, 4, 2, 128, 128], P('chain', 'grp'), may hold values from -1 to 1
- inverse_diag: float32 [16, 4, 128, 128], P('chain', 'grp'), as said below
- pattern: int32 [16, 4, 2], P('chain'), may hold values from 0 to 3, as said below
Outputs:
- forward_result: float32 [16, 4, 64, 128], P('chain', 'grp')
- solution: float32 [16, 4, 64, 128], P('chain', 'grp')
Inputs may be any that keep to these rules, and one draw needn't show every extreme that they name: `pattern`: the 2 entries of one supernode are different supernodes of the previous level. `inverse_diag`: every block is lower triangular with a diagonal between 0.75 and 1.05.
All inputs are finite; a program needn't handle non-finite values.
Results may differ from a plain program's by a relative error of at most 0.0002.
Values sent between devices are 32-bit elements; how exact they have to be, the bound alone decides.
No kernel may reach another device: no remote copies, remote signals or barrier semaphores. Data moves between devices by JAX's collectives and lax.ppermute only.
A program may use at most 320 MiB of HBM per device.

v0:
```python
import jax
import jax.numpy as jnp
from jax import lax
from jax.sharding import PartitionSpec as P

PRECISE = lax.Precision.HIGHEST


def matmul(left_side, right_factor):
    return jnp.dot(left_side, right_factor, precision=PRECISE, preferred_element_type=jnp.float32)


def matmul_trans(left_side, right_factor):
    return lax.dot_general(
        left_side,
        right_factor,
        (((1,), (1,)), ((), ())),
        precision=PRECISE,
        preferred_element_type=jnp.float32,
    )


def shards(right_side, factor, inverse_diag, pattern):
    levels = right_side.shape[0]
    samples = right_side.shape[2]
    sup_rows = right_side.shape[3]
    groups = lax.axis_size("grp")
    chain = lax.axis_size("chain")
    level_rows = groups * sup_rows
    my_group = lax.axis_index("grp")
    scaled = jnp.einsum(
        "lgti,lgkij->lgktj",
        inverse_diag,
        factor,
        precision=PRECISE,
        preferred_element_type=jnp.float32,
    )
    lifted = jnp.einsum(
        "lgsi,lgti->lgst",
        right_side,
        inverse_diag,
        precision=PRECISE,
        preferred_element_type=jnp.float32,
    )
    blocks, offsets = (
        lax.all_gather(scaled, "grp", axis=1, tiled=True),
        lax.all_gather(lifted, "grp", axis=1, tiled=True),
    )
    onehot = (pattern[..., None] == jnp.arange(groups, dtype=jnp.int32)).astype(jnp.float32)
    level_maps = -jnp.einsum(
        "lgkh,lgktj->lhjgt", onehot, blocks, precision=PRECISE, preferred_element_type=jnp.float32
    )
    level_maps = level_maps.reshape(levels, level_rows, level_rows)
    sources = offsets.transpose(0, 2, 1, 3).reshape(levels, samples, level_rows)

    def forward_levels(state):
        rows = []
        for level in range(levels):
            state = matmul(state, level_maps[level]) + sources[level]
            rows.append(state)
        return rows

    ahead = [(position, position + 1) for position in range(chain - 1)]
    behind = [(position + 1, position) for position in range(chain - 1)]

    def forward_hop(_, state):
        return lax.ppermute(forward_levels(state)[-1], "chain", ahead)

    incoming = jnp.zeros((samples, level_rows), jnp.float32)
    incoming = lax.fori_loop(0, chain - 1, forward_hop, incoming)
    solved = forward_levels(incoming)

    def backward_levels(running):
        rows = [None] * levels
        for level in reversed(range(levels)):
            rows[level] = solved[level] - running
            running = matmul_trans(-rows[level], level_maps[level])
        return (rows, running)

    def backward_hop(_, running):
        return lax.ppermute(backward_levels(running)[1], "chain", behind)

    arriving = jnp.zeros((samples, level_rows), jnp.float32)
    arriving = lax.fori_loop(0, chain - 1, backward_hop, arriving)
    pending_rows, _ = backward_levels(arriving)
    forward_own = []
    answers = []
    for level in range(levels):
        forward_own.append(
            lax.dynamic_slice_in_dim(solved[level], my_group * sup_rows, sup_rows, 1)
        )
        own_rows = lax.dynamic_slice_in_dim(pending_rows[level], my_group * sup_rows, sup_rows, 1)
        answers.append(matmul(own_rows, inverse_diag[level, 0]))
    forward_own = jnp.stack(forward_own)
    answers = jnp.stack(answers)
    return (forward_own[:, None], answers[:, None])


def solution(mesh):
    return jax.shard_map(
        shards,
        mesh=mesh,
        in_specs=(
            P("chain", "grp", None, None),
            P("chain", "grp", None, None, None),
            P("chain", "grp", None, None),
            P("chain", None, None),
        ),
        out_specs=(P("chain", "grp", None, None), P("chain", "grp", None, None)),
        check_vma=False,
    )
```

profile of v0, /device:TPU:0, one launch (start us, length us, event | category | flops | bytes accessed | tf_op | source)
XLA Modules:
  0.0 224.4 jit_solution(18291246836347683198)
XLA Ops:
  12.6 7.3 %all-gather = f32[2,256,128]{2,1,0:T(8,128)S(1)} all-gather(f32[2,64,128]{2,1,0:T(8,128)S(1)} %fusion.22), channel_id=2, replica_groups=mesh['chain'=8,'grp'=4] {'grp'}, dimensions={1}, use_global_device_ids=true | all-gather | bytes 327680 | tf_op jit(solution)/shard_map/all_gather | solution.py:47
  22.1 8.0 %all-gather.3.cloned.1.call-done = f32[2,4,2,128,128]{4,3,2,0,1:T(8,128)} async-done(((f32[2,1,2,128,128]{4,3,2,0,1:T(8,128)}), f32[2,4,2,128,128]{4,3,2,0,1:T(8,128)}) %all-gather.3.cloned.1.call-update) | async-done | bytes 1048592 | tf_op jit(solution)/shard_map/all_gather | solution.py:46
  30.1 3.9 %negate_bitcast_fusion = f32[2,4,128,4,128]{2,1,4,3,0:T(4,128)S(1)} fusion(f32[2,4,2,128,128]{4,3,2,0,1:T(8,128)} %all-gather.3.cloned.1.call-done, s32[2,4,2]{2,1,0:T(4,128)S(1)} %copy.17), kind=kOutput, calls=%fused_computation.15 | convolution fusion | flops 13107264 | bytes 3145792 | tf_op jit(solution)/shard_map/lgkh,lgktj->lhjgt/dot_general | solution.py:50
  38.9 80.6 %while.20 = (s32[]{:T(128)}, f32[64,512]{1,0:T(8,128)S(1)}, f32[2,512,512]{2,1,0:T(8,128)S(1)}, f32[2,64,512]{2,1,0:T(8,128)}, s32[]{:T(128)}) while((s32[]{:T(128)}, f32[64,512]{1,0:T(8,128)S(1)}, f32[2,512,512]{2,1,0:T(8,128)S(1)}, f32[2,64,512]{2,1,0:T(8,128)}, s32[]{:T(128)}) %tuple.53), condition=%wide.region_1.0_spmd, body=%wide.region_0.0_spmd.sunk | while | flops 402718720 | bytes 3407973 | solution.py:70
  40.6 2.3 %convolution_add_fusion.7 = f32[64,512]{1,0:T(8,128)} fusion(f32[64,512]{1,0:T(8,128)S(1)} %convolution_add_fusion.6, f32[2,512,512]{2,1,0:T(8,128)S(1)} %get-tuple-element.167, f32[2,64,512]{2,1,0:T(8,128)} %get-tuple-element.168), kind=kOutput, calls=%fused_computation.clone.1 | convolution fusion | flops 201359360 | bytes 1441792 | tf_op jit(solution)/shard_map/while/body/eval_jaxpr/dot_general | solution.py:10
  42.9 3.4 %collective-permute-start = (f32[64,512]{1,0:T(8,128)}, f32[64,512]{1,0:T(8,128)S(1)}, u32[]{:S(2)}, u32[]{:S(2)}) collective-permute-start(f32[64,512]{1,0:T(8,128)} %convolution_add_fusion.7), channel_id=1, source_target_pairs={{0,4},{4,8},{8,12},{12,16},{16,20},{20,24},{24,28},{1,5},{5,9},{9,... | collective-permute-start | bytes 393224 | tf_op jit(solution)/shard_map/while/body/eval_jaxpr/ppermute | solution.py:67
  46.3 3.4 %collective-permute-done = f32[64,512]{1,0:T(8,128)S(1)} collective-permute-done((f32[64,512]{1,0:T(8,128)}, f32[64,512]{1,0:T(8,128)S(1)}, u32[]{:S(2)}, u32[]{:S(2)}) %collective-permute-start) | collective-permute-done | bytes 131104 | tf_op jit(solution)/shard_map/while/body/eval_jaxpr/ppermute | solution.py:67
  51.4 2.3 %convolution_add_fusion.7 = f32[64,512]{1,0:T(8,128)} fusion(f32[64,512]{1,0:T(8,128)S(1)} %convolution_add_fusion.6, f32[2,512,512]{2,1,0:T(8,128)S(1)} %get-tuple-element.167, f32[2,64,512]{2,1,0:T(8,128)} %get-tuple-element.168), kind=kOutput, calls=%fused_computation.clone.1 | convolution fusion | flops 201359360 | bytes 1441792 | tf_op jit(solution)/shard_map/while/body/eval_jaxpr/dot_general | solution.py:10
  53.7 4.3 %collective-permute-start = (f32[64,512]{1,0:T(8,128)}, f32[64,512]{1,0:T(8,128)S(1)}, u32[]{:S(2)}, u32[]{:S(2)}) collective-permute-start(f32[64,512]{1,0:T(8,128)} %convolution_add_fusion.7), channel_id=1, source_target_pairs={{0,4},{4,8},{8,12},{12,16},{16,20},{20,24},{24,28},{1,5},{5,9},{9,... | collective-permute-start | bytes 393224 | tf_op jit(solution)/shard_map/while/body/eval_jaxpr/ppermute | solution.py:67
  57.9 2.8 %collective-permute-done = f32[64,512]{1,0:T(8,128)S(1)} collective-permute-done((f32[64,512]{1,0:T(8,128)}, f32[64,512]{1,0:T(8,128)S(1)}, u32[]{:S(2)}, u32[]{:S(2)}) %collective-permute-start) | collective-permute-done | bytes 131104 | tf_op jit(solution)/shard_map/while/body/eval_jaxpr/ppermute | solution.py:67
  64.7 4.3 %collective-permute-start = (f32[64,512]{1,0:T(8,128)}, f32[64,512]{1,0:T(8,128)S(1)}, u32[]{:S(2)}, u32[]{:S(2)}) collective-permute-start(f32[64,512]{1,0:T(8,128)} %convolution_add_fusion.7), channel_id=1, source_target_pairs={{0,4},{4,8},{8,12},{12,16},{16,20},{20,24},{24,28},{1,5},{5,9},{9,... | collective-permute-start | bytes 393224 | tf_op jit(solution)/shard_map/while/body/eval_jaxpr/ppermute | solution.py:67
  69.0 2.8 %collective-permute-done = f32[64,512]{1,0:T(8,128)S(1)} collective-permute-done((f32[64,512]{1,0:T(8,128)}, f32[64,512]{1,0:T(8,128)S(1)}, u32[]{:S(2)}, u32[]{:S(2)}) %collective-permute-start) | collective-permute-done | bytes 131104 | tf_op jit(solution)/shard_map/while/body/eval_jaxpr/ppermute | solution.py:67
  73.5 2.3 %convolution_add_fusion.7 = f32[64,512]{1,0:T(8,128)} fusion(f32[64,512]{1,0:T(8,128)S(1)} %convolution_add_fusion.6, f32[2,512,512]{2,1,0:T(8,128)S(1)} %get-tuple-element.167, f32[2,64,512]{2,1,0:T(8,128)} %get-tuple-element.168), kind=kOutput, calls=%fused_computation.clone.1 | convolution fusion | flops 201359360 | bytes 1441792 | tf_op jit(solution)/shard_map/while/body/eval_jaxpr/dot_general | solution.py:10
  75.8 5.1 %collective-permute-start = (f32[64,512]{1,0:T(8,128)}, f32[64,512]{1,0:T(8,128)S(1)}, u32[]{:S(2)}, u32[]{:S(2)}) collective-permute-start(f32[64,512]{1,0:T(8,128)} %convolution_add_fusion.7), channel_id=1, source_target_pairs={{0,4},{4,8},{8,12},{12,16},{16,20},{20,24},{24,28},{1,5},{5,9},{9,... | collective-permute-start | bytes 393224 | tf_op jit(solution)/shard_map/while/body/eval_jaxpr/ppermute | solution.py:67
  80.9 2.8 %collective-permute-done = f32[64,512]{1,0:T(8,128)S(1)} collective-permute-done((f32[64,512]{1,0:T(8,128)}, f32[64,512]{1,0:T(8,128)S(1)}, u32[]{:S(2)}, u32[]{:S(2)}) %collective-permute-start) | collective-permute-done | bytes 131104 | tf_op jit(solution)/shard_map/while/body/eval_jaxpr/ppermute | solution.py:67
  87.7 5.1 %collective-permute-start = (f32[64,512]{1,0:T(8,128)}, f32[64,512]{1,0:T(8,128)S(1)}, u32[]{:S(2)}, u32[]{:S(2)}) collective-permute-start(f32[64,512]{1,0:T(8,128)} %convolution_add_fusion.7), channel_id=1, source_target_pairs={{0,4},{4,8},{8,12},{12,16},{16,20},{20,24},{24,28},{1,5},{5,9},{9,... | collective-permute-start | bytes 393224 | tf_op jit(solution)/shard_map/while/body/eval_jaxpr/ppermute | solution.py:67
  92.8 2.8 %collective-permute-done = f32[64,512]{1,0:T(8,128)S(1)} collective-permute-done((f32[64,512]{1,0:T(8,128)}, f32[64,512]{1,0:T(8,128)S(1)}, u32[]{:S(2)}, u32[]{:S(2)}) %collective-permute-start) | collective-permute-done | bytes 131104 | tf_op jit(solution)/shard_map/while/body/eval_jaxpr/ppermute | solution.py:67
  99.6 5.1 %collective-permute-start = (f32[64,512]{1,0:T(8,128)}, f32[64,512]{1,0:T(8,128)S(1)}, u32[]{:S(2)}, u32[]{:S(2)}) collective-permute-start(f32[64,512]{1,0:T(8,128)} %convolution_add_fusion.7), channel_id=1, source_target_pairs={{0,4},{4,8},{8,12},{12,16},{16,20},{20,24},{24,28},{1,5},{5,9},{9,... | collective-permute-start | bytes 393224 | tf_op jit(solution)/shard_map/while/body/eval_jaxpr/ppermute | solution.py:67
  104.8 2.8 %collective-permute-done = f32[64,512]{1,0:T(8,128)S(1)} collective-permute-done((f32[64,512]{1,0:T(8,128)}, f32[64,512]{1,0:T(8,128)S(1)}, u32[]{:S(2)}, u32[]{:S(2)}) %collective-permute-start) | collective-permute-done | bytes 131104 | tf_op jit(solution)/shard_map/while/body/eval_jaxpr/ppermute | solution.py:67
  109.2 2.3 %convolution_add_fusion.7 = f32[64,512]{1,0:T(8,128)} fusion(f32[64,512]{1,0:T(8,128)S(1)} %convolution_add_fusion.6, f32[2,512,512]{2,1,0:T(8,128)S(1)} %get-tuple-element.167, f32[2,64,512]{2,1,0:T(8,128)} %get-tuple-element.168), kind=kOutput, calls=%fused_computation.clone.1 | convolution fusion | flops 201359360 | bytes 1441792 | tf_op jit(solution)/shard_map/while/body/eval_jaxpr/dot_general | solution.py:10
  111.5 5.1 %collective-permute-start = (f32[64,512]{1,0:T(8,128)}, f32[64,512]{1,0:T(8,128)S(1)}, u32[]{:S(2)}, u32[]{:S(2)}) collective-permute-start(f32[64,512]{1,0:T(8,128)} %convolution_add_fusion.7), channel_id=1, source_target_pairs={{0,4},{4,8},{8,12},{12,16},{16,20},{20,24},{24,28},{1,5},{5,9},{9,... | collective-permute-start | bytes 393224 | tf_op jit(solution)/shard_map/while/body/eval_jaxpr/ppermute | solution.py:67
  116.7 2.8 %collective-permute-done = f32[64,512]{1,0:T(8,128)S(1)} collective-permute-done((f32[64,512]{1,0:T(8,128)}, f32[64,512]{1,0:T(8,128)S(1)}, u32[]{:S(2)}, u32[]{:S(2)}) %collective-permute-start) | collective-permute-done | bytes 131104 | tf_op jit(solution)/shard_map/while/body/eval_jaxpr/ppermute | solution.py:67
  120.1 2.4 %convolution_add_fusion.3 = f32[64,512]{1,0:T(8,128)S(1)} fusion(f32[64,512]{1,0:T(8,128)} %copy-done.1, f32[64,8,4,128]{3,2,1,0:T(4,128)} %bitcast.120, f32[8,8,4,128]{3,2,1,0:T(4,128)} %bitcast.124), kind=kOutput, calls=%fused_computation.18 | convolution fusion | flops 201359360 | bytes 1441792 | tf_op jit(solution)/shard_map/dot_general | solution.py:10
  122.5 2.7 %convolution_add_fusion.2 = f32[64,512]{1,0:T(8,128)} fusion(f32[64,512]{1,0:T(8,128)S(1)} %convolution_add_fusion.3, f32[64,8,4,128]{3,2,1,0:T(4,128)S(1)} %bitcast.117, f32[8,8,4,128]{3,2,1,0:T(4,128)} %bitcast.123), kind=kOutput, calls=%fused_computation.17 | convolution fusion | flops 201359360 | bytes 1441792 | tf_op jit(solution)/shard_map/dot_general | solution.py:10
  125.8 85.9 %while.21 = (s32[]{:T(128)}, f32[64,512]{1,0:T(8,128)}, f32[64,512]{1,0:T(8,128)}, f32[2,512,512]{2,1,0:T(8,128)S(1)}, f32[64,512]{1,0:T(8,128)S(1)}, /*index=5*/s32[]{:T(128)}) while((s32[]{:T(128)}, f32[64,512]{1,0:T(8,128)}, f32[64,512]{1,0:T(8,128)}, f32[2,512,512]{2,1,0:T(8,128)S(1)}, f32[64,512]{1,0:T(8,128)S(1)}, ...), condition=%wide.region_3.0_spmd, body=%wide.region_2.0_spmd.sunk | while | flops 402784256 | bytes 3407981 | solution.py:84
  131.0 7.1 %collective-permute-done.1 = f32[64,512]{1,0:T(8,128)} collective-permute-done((f32[64,512]{1,0:T(8,128)}, f32[64,512]{1,0:T(8,128)}, u32[]{:S(2)}, u32[]{:S(2)}) %collective-permute-start.1) | collective-permute-done | bytes 131104 | tf_op jit(solution)/shard_map/while/body/eval_jaxpr/ppermute | solution.py:81
  143.2 7.1 %collective-permute-done.1 = f32[64,512]{1,0:T(8,128)} collective-permute-done((f32[64,512]{1,0:T(8,128)}, f32[64,512]{1,0:T(8,128)}, u32[]{:S(2)}, u32[]{:S(2)}) %collective-permute-start.1) | collective-permute-done | bytes 131104 | tf_op jit(solution)/shard_map/while/body/eval_jaxpr/ppermute | solution.py:81
  155.5 7.6 %collective-permute-done.1 = f32[64,512]{1,0:T(8,128)} collective-permute-done((f32[64,512]{1,0:T(8,128)}, f32[64,512]{1,0:T(8,128)}, u32[]{:S(2)}, u32[]{:S(2)}) %collective-permute-start.1) | collective-permute-done | bytes 131104 | tf_op jit(solution)/shard_map/while/body/eval_jaxpr/ppermute | solution.py:81
  168.3 7.9 %collective-permute-done.1 = f32[64,512]{1,0:T(8,128)} collective-permute-done((f32[64,512]{1,0:T(8,128)}, f32[64,512]{1,0:T(8,128)}, u32[]{:S(2)}, u32[]{:S(2)}) %collective-permute-start.1) | collective-permute-done | bytes 131104 | tf_op jit(solution)/shard_map/while/body/eval_jaxpr/ppermute | solution.py:81
  181.3 6.5 %collective-permute-done.1 = f32[64,512]{1,0:T(8,128)} collective-permute-done((f32[64,512]{1,0:T(8,128)}, f32[64,512]{1,0:T(8,128)}, u32[]{:S(2)}, u32[]{:S(2)}) %collective-permute-start.1) | collective-permute-done | bytes 131104 | tf_op jit(solution)/shard_map/while/body/eval_jaxpr/ppermute | solution.py:81
  193.0 6.8 %collective-permute-done.1 = f32[64,512]{1,0:T(8,128)} collective-permute-done((f32[64,512]{1,0:T(8,128)}, f32[64,512]{1,0:T(8,128)}, u32[]{:S(2)}, u32[]{:S(2)}) %collective-permute-start.1) | collective-permute-done | bytes 131104 | tf_op jit(solution)/shard_map/while/body/eval_jaxpr/ppermute | solution.py:81
  204.9 6.8 %collective-permute-done.1 = f32[64,512]{1,0:T(8,128)} collective-permute-done((f32[64,512]{1,0:T(8,128)}, f32[64,512]{1,0:T(8,128)}, u32[]{:S(2)}, u32[]{:S(2)}) %collective-permute-start.1) | collective-permute-done | bytes 131104 | tf_op jit(solution)/shard_map/while/body/eval_jaxpr/ppermute | solution.py:81
  (57 shorter events, 74.2 us)
Async XLA Ops:
  7.2 1.0 copy-start
  7.2 22.9 %all-gather.3.cloned.1.call-start = ((), (), s32[]{:S(2)}) async-start(), calls=%async_computation | async-start | bytes 1310720 | tf_op jit(solution)/shard_map/all_gather | solution.py:46
  42.9 6.8 %collective-permute-start = (f32[64,512]{1,0:T(8,128)}, f32[64,512]{1,0:T(8,128)S(1)}, u32[]{:S(2)}, u32[]{:S(2)}) collective-permute-start(f32[64,512]{1,0:T(8,128)} %convolution_add_fusion.7), channel_id=1, source_target_pairs={{0,4},{4,8},{8,12},{12,16},{16,20},{20,24},{24,28},{1,5},{5,9},{9,... | collective-permute-start | bytes 393224 | tf_op jit(solution)/shard_map/while/body/eval_jaxpr/ppermute | solution.py:67
  53.7 7.1 %collective-permute-start = (f32[64,512]{1,0:T(8,128)}, f32[64,512]{1,0:T(8,128)S(1)}, u32[]{:S(2)}, u32[]{:S(2)}) collective-permute-start(f32[64,512]{1,0:T(8,128)} %convolution_add_fusion.7), channel_id=1, source_target_pairs={{0,4},{4,8},{8,12},{12,16},{16,20},{20,24},{24,28},{1,5},{5,9},{9,... | collective-permute-start | bytes 393224 | tf_op jit(solution)/shard_map/while/body/eval_jaxpr/ppermute | solution.py:67
  64.7 7.1 %collective-permute-start = (f32[64,512]{1,0:T(8,128)}, f32[64,512]{1,0:T(8,128)S(1)}, u32[]{:S(2)}, u32[]{:S(2)}) collective-permute-start(f32[64,512]{1,0:T(8,128)} %convolution_add_fusion.7), channel_id=1, source_target_pairs={{0,4},{4,8},{8,12},{12,16},{16,20},{20,24},{24,28},{1,5},{5,9},{9,... | collective-permute-start | bytes 393224 | tf_op jit(solution)/shard_map/while/body/eval_jaxpr/ppermute | solution.py:67
  75.8 8.0 %collective-permute-start = (f32[64,512]{1,0:T(8,128)}, f32[64,512]{1,0:T(8,128)S(1)}, u32[]{:S(2)}, u32[]{:S(2)}) collective-permute-start(f32[64,512]{1,0:T(8,128)} %convolution_add_fusion.7), channel_id=1, source_target_pairs={{0,4},{4,8},{8,12},{12,16},{16,20},{20,24},{24,28},{1,5},{5,9},{9,... | collective-permute-start | bytes 393224 | tf_op jit(solution)/shard_map/while/body/eval_jaxpr/ppermute | solution.py:67
  87.7 8.0 %collective-permute-start = (f32[64,512]{1,0:T(8,128)}, f32[64,512]{1,0:T(8,128)S(1)}, u32[]{:S(2)}, u32[]{:S(2)}) collective-permute-start(f32[64,512]{1,0:T(8,128)} %convolution_add_fusion.7), channel_id=1, source_target_pairs={{0,4},{4,8},{8,12},{12,16},{16,20},{20,24},{24,28},{1,5},{5,9},{9,... | collective-permute-start | bytes 393224 | tf_op jit(solution)/shard_map/while/body/eval_jaxpr/ppermute | solution.py:67
  99.6 8.0 %collective-permute-start = (f32[64,512]{1,0:T(8,128)}, f32[64,512]{1,0:T(8,128)S(1)}, u32[]{:S(2)}, u32[]{:S(2)}) collective-permute-start(f32[64,512]{1,0:T(8,128)} %convolution_add_fusion.7), channel_id=1, source_target_pairs={{0,4},{4,8},{8,12},{12,16},{16,20},{20,24},{24,28},{1,5},{5,9},{9,... | collective-permute-start | bytes 393224 | tf_op jit(solution)/shard_map/while/body/eval_jaxpr/ppermute | solution.py:67
  111.5 8.0 %collective-permute-start = (f32[64,512]{1,0:T(8,128)}, f32[64,512]{1,0:T(8,128)S(1)}, u32[]{:S(2)}, u32[]{:S(2)}) collective-permute-start(f32[64,512]{1,0:T(8,128)} %convolution_add_fusion.7), channel_id=1, source_target_pairs={{0,4},{4,8},{8,12},{12,16},{16,20},{20,24},{24,28},{1,5},{5,9},{9,... | collective-permute-start | bytes 393224 | tf_op jit(solution)/shard_map/while/body/eval_jaxpr/ppermute | solution.py:67
  119.5 0.6 copy-start.1
  129.7 8.4 %collective-permute-start.1 = (f32[64,512]{1,0:T(8,128)}, f32[64,512]{1,0:T(8,128)}, u32[]{:S(2)}, u32[]{:S(2)}) collective-permute-start(f32[64,512]{1,0:T(8,128)} %fusion.64), channel_id=1, source_target_pairs={{4,0},{8,4},{12,8},{16,12},{20,16},{24,20},{28,24},{5,1},{9,5},{13... | collective-permute-start | bytes 393224 | tf_op jit(solution)/shard_map/while/body/eval_jaxpr/ppermute | solution.py:81
  142.0 8.4 %collective-permute-start.1 = (f32[64,512]{1,0:T(8,128)}, f32[64,512]{1,0:T(8,128)}, u32[]{:S(2)}, u32[]{:S(2)}) collective-permute-start(f32[64,512]{1,0:T(8,128)} %fusion.64), channel_id=1, source_target_pairs={{4,0},{8,4},{12,8},{16,12},{20,16},{24,20},{28,24},{5,1},{9,5},{13... | collective-permute-start | bytes 393224 | tf_op jit(solution)/shard_map/while/body/eval_jaxpr/ppermute | solution.py:81
  154.2 8.9 %collective-permute-start.1 = (f32[64,512]{1,0:T(8,128)}, f32[64,512]{1,0:T(8,128)}, u32[]{:S(2)}, u32[]{:S(2)}) collective-permute-start(f32[64,512]{1,0:T(8,128)} %fusion.64), channel_id=1, source_target_pairs={{4,0},{8,4},{12,8},{16,12},{20,16},{24,20},{28,24},{5,1},{9,5},{13... | collective-permute-start | bytes 393224 | tf_op jit(solution)/shard_map/while/body/eval_jaxpr/ppermute | solution.py:81
  167.0 9.2 %collective-permute-start.1 = (f32[64,512]{1,0:T(8,128)}, f32[64,512]{1,0:T(8,128)}, u32[]{:S(2)}, u32[]{:S(2)}) collective-permute-start(f32[64,512]{1,0:T(8,128)} %fusion.64), channel_id=1, source_target_pairs={{4,0},{8,4},{12,8},{16,12},{20,16},{24,20},{28,24},{5,1},{9,5},{13... | collective-permute-start | bytes 393224 | tf_op jit(solution)/shard_map/while/body/eval_jaxpr/ppermute | solution.py:81
  180.1 7.8 %collective-permute-start.1 = (f32[64,512]{1,0:T(8,128)}, f32[64,512]{1,0:T(8,128)}, u32[]{:S(2)}, u32[]{:S(2)}) collective-permute-start(f32[64,512]{1,0:T(8,128)} %fusion.64), channel_id=1, source_target_pairs={{4,0},{8,4},{12,8},{16,12},{20,16},{24,20},{28,24},{5,1},{9,5},{13... | collective-permute-start | bytes 393224 | tf_op jit(solution)/shard_map/while/body/eval_jaxpr/ppermute | solution.py:81
  191.7 8.1 %collective-permute-start.1 = (f32[64,512]{1,0:T(8,128)}, f32[64,512]{1,0:T(8,128)}, u32[]{:S(2)}, u32[]{:S(2)}) collective-permute-start(f32[64,512]{1,0:T(8,128)} %fusion.64), channel_id=1, source_target_pairs={{4,0},{8,4},{12,8},{16,12},{20,16},{24,20},{28,24},{5,1},{9,5},{13... | collective-permute-start | bytes 393224 | tf_op jit(solution)/shard_map/while/body/eval_jaxpr/ppermute | solution.py:81
  203.6 8.1 %collective-permute-start.1 = (f32[64,512]{1,0:T(8,128)}, f32[64,512]{1,0:T(8,128)}, u32[]{:S(2)}, u32[]{:S(2)}) collective-permute-start(f32[64,512]{1,0:T(8,128)} %fusion.64), channel_id=1, source_target_pairs={{4,0},{8,4},{12,8},{16,12},{20,16},{24,20},{28,24},{5,1},{9,5},{13... | collective-permute-start | bytes 393224 | tf_op jit(solution)/shard_map/while/body/eval_jaxpr/ppermute | solution.py:81
Sparse Core Ops, SparseCore 0:
  10.6 19.4 all-gather.2
where the time goes:
time: 226 us; the launch traced here: 224 us
  waiting for transfers between devices  78.1 us (35%)
  matrix products  69.3 us (31%)
  starting transfers between devices  41.5 us (18%)
  between operations  14.1 us (6%)
  local copies, waits for them, and re-layouts  11.8 us (5%)
  blocking collectives  7.25 us (3%)
    ppermute x7, waiting for transfers between devices, backward_hop(): return lax.ppermute(backward_levels(running)[1], 'chain', behind)  49.8 us
    dot_general x18, matrix products, matmul(): jnp.dot(left_side, right_factor, precision=PRECISE, preferred_element_typ...  34.8 us
    ppermute x7, starting transfers between devices, forward_hop(): return lax.ppermute(forward_levels(state)[-1], 'chain', ahead)  32.5 us
    dot_general x15, matrix products, matmul_trans(): lax.dot_general(left_side, right_factor, (((1,), (1,)), ((), ())), precis...  27.8 us
    ppermute x7, waiting for transfers between devices, forward_hop(): return lax.ppermute(forward_levels(state)[-1], 'chain', ahead)  20.3 us
    ppermute x7, starting transfers between devices, backward_hop(): return lax.ppermute(backward_levels(running)[1], 'chain', behind)  8.96 us
    all_gather x1, waiting for transfers between devices, shards(): lax.all_gather(scaled, 'grp', axis=1, tiled=True)  8 us
    all_gather x1, blocking collectives, shards(): lax.all_gather(lifted, 'grp', axis=1, tiled=True)  7.25 us
  transfers between devices with their start and end apart: 15, of which 15 were waited for; matrix products, arithmetic and copies ran while one was open for 2% of the time, Pallas kernels for 0%

commit v1 on v0

--- a/solution.py
+++ b/solution.py
@@ -4,6 +4,28 @@
 from jax.sharding import PartitionSpec as P
 
 PRECISE = lax.Precision.HIGHEST
+
+
+def in_order(parts, dim):
+    lengths = list(parts.shape[1:])
+    lengths[dim] *= parts.shape[0]
+    return jnp.moveaxis(parts, 0, dim).reshape(lengths)
+
+
+def ring_gather(x, axis, dim):
+    size = lax.axis_size(axis)
+    pairs = [(i, (i + 1) % size) for i in range(size)]
+    back = [(b, a) for a, b in pairs]
+    lower, upper = ([], [])
+    for step in range(size - 1):
+        if step % 2 == 0:
+            lower.append(lax.ppermute(lower[-1] if lower else x, axis, pairs))
+        else:
+            upper.append(lax.ppermute(upper[-1] if upper else x, axis, back))
+    blocks = jnp.stack([*lower[::-1], x, *upper])
+    shift = lax.axis_index(axis) - len(lower)
+    blocks = blocks[(jnp.arange(size) - shift) % size]
+    return in_order(blocks, dim)
 
 
 def matmul(left_side, right_factor):
@@ -43,7 +65,7 @@
         preferred_element_type=jnp.float32,
     )
     blocks, offsets = (
-        lax.all_gather(scaled, "grp", axis=1, tiled=True),
+        ring_gather(scaled, "grp", 1),
         lax.all_gather(lifted, "grp", axis=1, tiled=True),
     )
     onehot = (pattern[..., None] == jnp.arange(groups, dtype=jnp.int32)).astype(jnp.float32)

time: 226 us -> 209 us (0.925)
  between operations: 14.1 us -> 0.75 us
  waiting for transfers between devices: 78.1 us -> 72.6 us
  starting transfers between devices: 41.5 us -> 44.7 us
    all_gather x1 -> x0, waiting for transfers between devices: 8 us -> none  [shards(): lax.all_gather(scaled, 'grp', axis=1, tiled=True)]
    ppermute x0 -> x3, waiting for transfers between devices: none -> 2.91 us  [the longest x2 2.9 us: ring_gather(): lower.append(lax.ppermute(lower[-1] if lower else x, axis, pairs))]
    ppermute x0 -> x3, starting transfers between devices: none -> 2.9 us  [the longest x1 2.01 us: ring_gather(): upper.append(lax.ppermute(upper[-1] if upper else x, axis, back))]
  transfers between devices with their start and end apart: 15 -> 17, of which waited for: 15 -> 15; matrix products, arithmetic and copies ran while one was open for 2% -> 2% of each run, Pallas kernels for 0% -> 0%
where the time goes in v1:
time: 209 us; the launch traced here: 208 us
  waiting for transfers between devices  72.6 us (35%)
  matrix products  67.7 us (32%)
  starting transfers between devices  44.7 us (21%)
  local copies, waits for them, and re-layouts  12.2 us (6%)
  blocking collectives  7.74 us (4%)
  other arithmetic  2.37 us (1%)
    ppermute x7, waiting for transfers between devices, backward_hop(): return lax.ppermute(backward_levels(running)[1], 'chain', behind)  50 us
    dot_general x18, matrix products, matmul(): jnp.dot(left_side, right_factor, precision=PRECISE, preferred_element_typ...  34.8 us
    ppermute x7, starting transfers between devices, forward_hop(): return lax.ppermute(forward_levels(state)[-1], 'chain', ahead)  32.8 us
    dot_general x15, matrix products, matmul_trans(): lax.dot_general(left_side, right_factor, (((1,), (1,)), ((), ())), precis...  27.8 us
    ppermute x7, waiting for transfers between devices, forward_hop(): return lax.ppermute(forward_levels(state)[-1], 'chain', ahead)  19.7 us
    ppermute x7, starting transfers between devices, backward_hop(): return lax.ppermute(backward_levels(running)[1], 'chain', behind)  8.96 us
    all_gather x1, blocking collectives, shards(): lax.all_gather(lifted, 'grp', axis=1, tiled=True)  7.74 us
  transfers between devices with their start and end apart: 17, of which 15 were waited for; matrix products, arithmetic and copies ran while one was open for 2% of the time, Pallas kernels for 0%

profile of v1, /device:TPU:0, one launch (start us, length us, event | category | flops | bytes accessed | tf_op | source)
XLA Modules:
  0.0 208.3 jit_solution(10255835644407514875)
XLA Ops:
  6.9 7.7 %all-gather = f32[2,256,128]{2,1,0:T(8,128)S(1)} all-gather(f32[2,64,128]{2,1,0:T(8,128)S(1)} %fusion.22), channel_id=2, replica_groups=mesh['chain'=8,'grp'=4] {'grp'}, dimensions={1}, use_global_device_ids=true | all-gather | bytes 327680 | tf_op jit(solution)/shard_map/all_gather | solution.py:69
  18.1 2.9 %collective-permute-done.3 = f32[2,1,2,128,128]{3,4,2,0,1:T(8,128)S(1)} collective-permute-done((f32[2,1,2,128,128]{3,4,2,0,1:T(8,128)S(1)}, f32[2,1,2,128,128]{3,4,2,0,1:T(8,128)S(1)}, u32[]{:S(2)}, u32[]{:S(2)}) %collective-permute-start.3) | collective-permute-done | bytes 262176 | tf_op jit(solution)/shard_map/ppermute | solution.py:22
  22.3 2.4 %negate_bitcast_fusion = f32[2,4,128,4,128]{2,1,4,3,0:T(4,128)S(1)} fusion(f32[2,4,2,128,128]{4,2,3,1,0:T(2,128)S(1)} %copy.8, s32[2,4,2]{2,1,0:T(4,128)S(1)} %copy.7), kind=kOutput, calls=%fused_computation.16 | convolution fusion | flops 13107264 | bytes 3145792 | tf_op jit(solution)/shard_map/lgkh,lgktj->lhjgt/dot_general | solution.py:72
  29.7 80.3 %while.20 = (s32[]{:T(128)}, f32[64,512]{1,0:T(8,128)S(1)}, f32[2,512,512]{2,1,0:T(8,128)S(1)}, f32[2,64,512]{2,1,0:T(8,128)}, s32[]{:T(128)}) while((s32[]{:T(128)}, f32[64,512]{1,0:T(8,128)S(1)}, f32[2,512,512]{2,1,0:T(8,128)S(1)}, f32[2,64,512]{2,1,0:T(8,128)}, s32[]{:T(128)}) %tuple.48), condition=%wide.region_1.2_spmd, body=%wide.region_0.1_spmd.sunk | while | flops 402718720 | bytes 3407973 | solution.py:92
  33.6 3.7 %collective-permute-start = (f32[64,512]{1,0:T(8,128)}, f32[64,512]{1,0:T(8,128)S(1)}, u32[]{:S(2)}, u32[]{:S(2)}) collective-permute-start(f32[64,512]{1,0:T(8,128)} %convolution_add_fusion.7), channel_id=1, source_target_pairs={{0,4},{4,8},{8,12},{12,16},{16,20},{20,24},{24,28},{1,5},{5,9},{9,... | collective-permute-start | bytes 393224 | tf_op jit(solution)/shard_map/while/body/eval_jaxpr/ppermute | solution.py:89
  37.3 2.8 %collective-permute-done = f32[64,512]{1,0:T(8,128)S(1)} collective-permute-done((f32[64,512]{1,0:T(8,128)}, f32[64,512]{1,0:T(8,128)S(1)}, u32[]{:S(2)}, u32[]{:S(2)}) %collective-permute-start) | collective-permute-done | bytes 131104 | tf_op jit(solution)/shard_map/while/body/eval_jaxpr/ppermute | solution.py:89
  41.8 2.3 %convolution_add_fusion.7 = f32[64,512]{1,0:T(8,128)} fusion(f32[64,512]{1,0:T(8,128)S(1)} %convolution_add_fusion.6, f32[2,512,512]{2,1,0:T(8,128)S(1)} %get-tuple-element.156, f32[2,64,512]{2,1,0:T(8,128)} %get-tuple-element.157), kind=kOutput, calls=%fused_computation.1.clone.1 | convolution fusion | flops 201359360 | bytes 1441792 | tf_op jit(solution)/shard_map/while/body/eval_jaxpr/dot_general | solution.py:32
  44.1 4.2 %collective-permute-start = (f32[64,512]{1,0:T(8,128)}, f32[64,512]{1,0:T(8,128)S(1)}, u32[]{:S(2)}, u32[]{:S(2)}) collective-permute-start(f32[64,512]{1,0:T(8,128)} %convolution_add_fusion.7), channel_id=1, source_target_pairs={{0,4},{4,8},{8,12},{12,16},{16,20},{20,24},{24,28},{1,5},{5,9},{9,... | collective-permute-start | bytes 393224 | tf_op jit(solution)/shard_map/while/body/eval_jaxpr/ppermute | solution.py:89
  48.3 2.8 %collective-permute-done = f32[64,512]{1,0:T(8,128)S(1)} collective-permute-done((f32[64,512]{1,0:T(8,128)}, f32[64,512]{1,0:T(8,128)S(1)}, u32[]{:S(2)}, u32[]{:S(2)}) %collective-permute-start) | collective-permute-done | bytes 131104 | tf_op jit(solution)/shard_map/while/body/eval_jaxpr/ppermute | solution.py:89
  52.8 2.3 %convolution_add_fusion.7 = f32[64,512]{1,0:T(8,128)} fusion(f32[64,512]{1,0:T(8,128)S(1)} %convolution_add_fusion.6, f32[2,512,512]{2,1,0:T(8,128)S(1)} %get-tuple-element.156, f32[2,64,512]{2,1,0:T(8,128)} %get-tuple-element.157), kind=kOutput, calls=%fused_computation.1.clone.1 | convolution fusion | flops 201359360 | bytes 1441792 | tf_op jit(solution)/shard_map/while/body/eval_jaxpr/dot_general | solution.py:32
  55.1 4.3 %collective-permute-start = (f32[64,512]{1,0:T(8,128)}, f32[64,512]{1,0:T(8,128)S(1)}, u32[]{:S(2)}, u32[]{:S(2)}) collective-permute-start(f32[64,512]{1,0:T(8,128)} %convolution_add_fusion.7), channel_id=1, source_target_pairs={{0,4},{4,8},{8,12},{12,16},{16,20},{20,24},{24,28},{1,5},{5,9},{9,... | collective-permute-start | bytes 393224 | tf_op jit(solution)/shard_map/while/body/eval_jaxpr/ppermute | solution.py:89
  59.4 2.8 %collective-permute-done = f32[64,512]{1,0:T(8,128)S(1)} collective-permute-done((f32[64,512]{1,0:T(8,128)}, f32[64,512]{1,0:T(8,128)S(1)}, u32[]{:S(2)}, u32[]{:S(2)}) %collective-permute-start) | collective-permute-done | bytes 131104 | tf_op jit(solution)/shard_map/while/body/eval_jaxpr/ppermute | solution.py:89
  63.9 2.3 %convolution_add_fusion.7 = f32[64,512]{1,0:T(8,128)} fusion(f32[64,512]{1,0:T(8,128)S(1)} %convolution_add_fusion.6, f32[2,512,512]{2,1,0:T(8,128)S(1)} %get-tuple-element.156, f32[2,64,512]{2,1,0:T(8,128)} %get-tuple-element.157), kind=kOutput, calls=%fused_computation.1.clone.1 | convolution fusion | flops 201359360 | bytes 1441792 | tf_op jit(solution)/shard_map/while/body/eval_jaxpr/dot_general | solution.py:32
  66.2 5.1 %collective-permute-start = (f32[64,512]{1,0:T(8,128)}, f32[64,512]{1,0:T(8,128)S(1)}, u32[]{:S(2)}, u32[]{:S(2)}) collective-permute-start(f32[64,512]{1,0:T(8,128)} %convolution_add_fusion.7), channel_id=1, source_target_pairs={{0,4},{4,8},{8,12},{12,16},{16,20},{20,24},{24,28},{1,5},{5,9},{9,... | collective-permute-start | bytes 393224 | tf_op jit(solution)/shard_map/while/body/eval_jaxpr/ppermute | solution.py:89
  71.4 2.8 %collective-permute-done = f32[64,512]{1,0:T(8,128)S(1)} collective-permute-done((f32[64,512]{1,0:T(8,128)}, f32[64,512]{1,0:T(8,128)S(1)}, u32[]{:S(2)}, u32[]{:S(2)}) %collective-permute-start) | collective-permute-done | bytes 131104 | tf_op jit(solution)/shard_map/while/body/eval_jaxpr/ppermute | solution.py:89
  78.1 5.1 %collective-permute-start = (f32[64,512]{1,0:T(8,128)}, f32[64,512]{1,0:T(8,128)S(1)}, u32[]{:S(2)}, u32[]{:S(2)}) collective-permute-start(f32[64,512]{1,0:T(8,128)} %convolution_add_fusion.7), channel_id=1, source_target_pairs={{0,4},{4,8},{8,12},{12,16},{16,20},{20,24},{24,28},{1,5},{5,9},{9,... | collective-permute-start | bytes 393224 | tf_op jit(solution)/shard_map/while/body/eval_jaxpr/ppermute | solution.py:89
  83.3 2.8 %collective-permute-done = f32[64,512]{1,0:T(8,128)S(1)} collective-permute-done((f32[64,512]{1,0:T(8,128)}, f32[64,512]{1,0:T(8,128)S(1)}, u32[]{:S(2)}, u32[]{:S(2)}) %collective-permute-start) | collective-permute-done | bytes 131104 | tf_op jit(solution)/shard_map/while/body/eval_jaxpr/ppermute | solution.py:89
  90.1 5.1 %collective-permute-start = (f32[64,512]{1,0:T(8,128)}, f32[64,512]{1,0:T(8,128)S(1)}, u32[]{:S(2)}, u32[]{:S(2)}) collective-permute-start(f32[64,512]{1,0:T(8,128)} %convolution_add_fusion.7), channel_id=1, source_target_pairs={{0,4},{4,8},{8,12},{12,16},{16,20},{20,24},{24,28},{1,5},{5,9},{9,... | collective-permute-start | bytes 393224 | tf_op jit(solution)/shard_map/while/body/eval_jaxpr/ppermute | solution.py:89
  95.2 2.8 %collective-permute-done = f32[64,512]{1,0:T(8,128)S(1)} collective-permute-done((f32[64,512]{1,0:T(8,128)}, f32[64,512]{1,0:T(8,128)S(1)}, u32[]{:S(2)}, u32[]{:S(2)}) %collective-permute-start) | collective-permute-done | bytes 131104 | tf_op jit(solution)/shard_map/while/body/eval_jaxpr/ppermute | solution.py:89
  99.7 2.3 %convolution_add_fusion.7 = f32[64,512]{1,0:T(8,128)} fusion(f32[64,512]{1,0:T(8,128)S(1)} %convolution_add_fusion.6, f32[2,512,512]{2,1,0:T(8,128)S(1)} %get-tuple-element.156, f32[2,64,512]{2,1,0:T(8,128)} %get-tuple-element.157), kind=kOutput, calls=%fused_computation.1.clone.1 | convolution fusion | flops 201359360 | bytes 1441792 | tf_op jit(solution)/shard_map/while/body/eval_jaxpr/dot_general | solution.py:32
  102.0 5.1 %collective-permute-start = (f32[64,512]{1,0:T(8,128)}, f32[64,512]{1,0:T(8,128)S(1)}, u32[]{:S(2)}, u32[]{:S(2)}) collective-permute-start(f32[64,512]{1,0:T(8,128)} %convolution_add_fusion.7), channel_id=1, source_target_pairs={{0,4},{4,8},{8,12},{12,16},{16,20},{20,24},{24,28},{1,5},{5,9},{9,... | collective-permute-start | bytes 393224 | tf_op jit(solution)/shard_map/while/body/eval_jaxpr/ppermute | solution.py:89
  107.1 2.8 %collective-permute-done = f32[64,512]{1,0:T(8,128)S(1)} collective-permute-done((f32[64,512]{1,0:T(8,128)}, f32[64,512]{1,0:T(8,128)S(1)}, u32[]{:S(2)}, u32[]{:S(2)}) %collective-permute-start) | collective-permute-done | bytes 131104 | tf_op jit(solution)/shard_map/while/body/eval_jaxpr/ppermute | solution.py:89
  110.6 2.4 %convolution_add_fusion.3 = f32[64,512]{1,0:T(8,128)S(1)} fusion(f32[64,512]{1,0:T(8,128)} %copy-done.1, f32[64,8,4,128]{3,2,1,0:T(4,128)} %bitcast.135, f32[8,8,4,128]{3,2,1,0:T(4,128)} %bitcast.142), kind=kOutput, calls=%fused_computation.18 | convolution fusion | flops 201359360 | bytes 1441792 | tf_op jit(solution)/shard_map/dot_general | solution.py:32
  112.9 2.7 %convolution_add_fusion.2 = f32[64,512]{1,0:T(8,128)} fusion(f32[64,512]{1,0:T(8,128)S(1)} %convolution_add_fusion.3, f32[64,8,4,128]{3,2,1,0:T(4,128)S(1)} %bitcast.131, f32[8,8,4,128]{3,2,1,0:T(4,128)} %bitcast.141), kind=kOutput, calls=%fused_computation.17 | convolution fusion | flops 201359360 | bytes 1441792 | tf_op jit(solution)/shard_map/dot_general | solution.py:32
  116.3 86.2 %while.21 = (s32[]{:T(128)}, f32[64,512]{1,0:T(8,128)}, f32[64,512]{1,0:T(8,128)}, f32[2,512,512]{2,1,0:T(8,128)S(1)}, f32[64,512]{1,0:T(8,128)S(1)}, /*index=5*/s32[]{:T(128)}) while((s32[]{:T(128)}, f32[64,512]{1,0:T(8,128)}, f32[64,512]{1,0:T(8,128)}, f32[2,512,512]{2,1,0:T(8,128)S(1)}, f32[64,512]{1,0:T(8,128)S(1)}, ...), condition=%wide.region_3.4_spmd, body=%wide.region_2.3_spmd.sunk | while | flops 402784256 | bytes 3407981 | solution.py:106
  121.4 7.1 %collective-permute-done.1 = f32[64,512]{1,0:T(8,128)} collective-permute-done((f32[64,512]{1,0:T(8,128)}, f32[64,512]{1,0:T(8,128)}, u32[]{:S(2)}, u32[]{:S(2)}) %collective-permute-start.1) | collective-permute-done | bytes 131104 | tf_op jit(solution)/shard_map/while/body/eval_jaxpr/ppermute | solution.py:103
  133.7 8.4 %collective-permute-done.1 = f32[64,512]{1,0:T(8,128)} collective-permute-done((f32[64,512]{1,0:T(8,128)}, f32[64,512]{1,0:T(8,128)}, u32[]{:S(2)}, u32[]{:S(2)}) %collective-permute-start.1) | collective-permute-done | bytes 131104 | tf_op jit(solution)/shard_map/while/body/eval_jaxpr/ppermute | solution.py:103
  147.2 7.7 %collective-permute-done.1 = f32[64,512]{1,0:T(8,128)} collective-permute-done((f32[64,512]{1,0:T(8,128)}, f32[64,512]{1,0:T(8,128)}, u32[]{:S(2)}, u32[]{:S(2)}) %collective-permute-start.1) | collective-permute-done | bytes 131104 | tf_op jit(solution)/shard_map/while/body/eval_jaxpr/ppermute | solution.py:103
  160.1 6.5 %collective-permute-done.1 = f32[64,512]{1,0:T(8,128)} collective-permute-done((f32[64,512]{1,0:T(8,128)}, f32[64,512]{1,0:T(8,128)}, u32[]{:S(2)}, u32[]{:S(2)}) %collective-permute-start.1) | collective-permute-done | bytes 131104 | tf_op jit(solution)/shard_map/while/body/eval_jaxpr/ppermute | solution.py:103
  171.8 6.8 %collective-permute-done.1 = f32[64,512]{1,0:T(8,128)} collective-permute-done((f32[64,512]{1,0:T(8,128)}, f32[64,512]{1,0:T(8,128)}, u32[]{:S(2)}, u32[]{:S(2)}) %collective-permute-start.1) | collective-permute-done | bytes 131104 | tf_op jit(solution)/shard_map/while/body/eval_jaxpr/ppermute | solution.py:103
  183.7 6.8 %collective-permute-done.1 = f32[64,512]{1,0:T(8,128)} collective-permute-done((f32[64,512]{1,0:T(8,128)}, f32[64,512]{1,0:T(8,128)}, u32[]{:S(2)}, u32[]{:S(2)}) %collective-permute-start.1) | collective-permute-done | bytes 131104 | tf_op jit(solution)/shard_map/while/body/eval_jaxpr/ppermute | solution.py:103
  195.7 6.8 %collective-permute-done.1 = f32[64,512]{1,0:T(8,128)} collective-permute-done((f32[64,512]{1,0:T(8,128)}, f32[64,512]{1,0:T(8,128)}, u32[]{:S(2)}, u32[]{:S(2)}) %collective-permute-start.1) | collective-permute-done | bytes 131104 | tf_op jit(solution)/shard_map/while/body/eval_jaxpr/ppermute | solution.py:103
  (64 shorter events, 77.6 us)
Async XLA Ops:
  0.6 1.0 copy-start
  3.1 11.6 %collective-permute-start.2 = (f32[2,1,2,128,128]{3,4,2,0,1:T(8,128)S(1)}, f32[2,1,2,128,128]{3,4,2,0,1:T(8,128)S(1)}, u32[]{:S(2)}, u32[]{:S(2)}) collective-permute-start(f32[2,1,2,128,128]{3,4,2,0,1:T(8,128)S(1)} %bitcast.138), channel_id=1, source_target_pairs={{0,1},{1,2},{2,3},{3,0},{4,5},{5,6},{6,7},{7,4},{8,9},{9,10},{10,1... | collective-permute-start | bytes 786440 | tf_op jit(solution)/shard_map/ppermute | solution.py:22
  3.6 14.5 %collective-permute-start.4 = (f32[2,1,2,128,128]{3,4,2,0,1:T(8,128)S(1)}, f32[2,1,2,128,128]{3,4,2,0,1:T(8,128)S(1)}, u32[]{:S(2)}, u32[]{:S(2)}) collective-permute-start(f32[2,1,2,128,128]{3,4,2,0,1:T(8,128)S(1)} %bitcast.139), channel_id=1, source_target_pairs={{1,0},{2,1},{3,2},{0,3},{5,4},{6,5},{7,6},{4,7},{9,8},{10,9},{11,1... | collective-permute-start | bytes 786440 | tf_op jit(solution)/shard_map/ppermute | solution.py:24
  14.7 6.3 %collective-permute-start.3 = (f32[2,1,2,128,128]{3,4,2,0,1:T(8,128)S(1)}, f32[2,1,2,128,128]{3,4,2,0,1:T(8,128)S(1)}, u32[]{:S(2)}, u32[]{:S(2)}) collective-permute-start(f32[2,1,2,128,128]{3,4,2,0,1:T(8,128)S(1)} %collective-permute-done.2), channel_id=1, source_target_pairs={{0,1},{1,2},{2,3},{3,0},{4,5},{5,6},{6,7},{7,4},{8,9},{9,10},{10,1... | collective-permute-start | bytes 786440 | tf_op jit(solution)/shard_map/ppermute | solution.py:22
  33.6 6.5 %collective-permute-start = (f32[64,512]{1,0:T(8,128)}, f32[64,512]{1,0:T(8,128)S(1)}, u32[]{:S(2)}, u32[]{:S(2)}) collective-permute-start(f32[64,512]{1,0:T(8,128)} %convolution_add_fusion.7), channel_id=1, source_target_pairs={{0,4},{4,8},{8,12},{12,16},{16,20},{20,24},{24,28},{1,5},{5,9},{9,... | collective-permute-start | bytes 393224 | tf_op jit(solution)/shard_map/while/body/eval_jaxpr/ppermute | solution.py:89
  44.1 7.1 %collective-permute-start = (f32[64,512]{1,0:T(8,128)}, f32[64,512]{1,0:T(8,128)S(1)}, u32[]{:S(2)}, u32[]{:S(2)}) collective-permute-start(f32[64,512]{1,0:T(8,128)} %convolution_add_fusion.7), channel_id=1, source_target_pairs={{0,4},{4,8},{8,12},{12,16},{16,20},{20,24},{24,28},{1,5},{5,9},{9,... | collective-permute-start | bytes 393224 | tf_op jit(solution)/shard_map/while/body/eval_jaxpr/ppermute | solution.py:89
  55.1 7.2 %collective-permute-start = (f32[64,512]{1,0:T(8,128)}, f32[64,512]{1,0:T(8,128)S(1)}, u32[]{:S(2)}, u32[]{:S(2)}) collective-permute-start(f32[64,512]{1,0:T(8,128)} %convolution_add_fusion.7), channel_id=1, source_target_pairs={{0,4},{4,8},{8,12},{12,16},{16,20},{20,24},{24,28},{1,5},{5,9},{9,... | collective-permute-start | bytes 393224 | tf_op jit(solution)/shard_map/while/body/eval_jaxpr/ppermute | solution.py:89
  66.2 8.0 %collective-permute-start = (f32[64,512]{1,0:T(8,128)}, f32[64,512]{1,0:T(8,128)S(1)}, u32[]{:S(2)}, u32[]{:S(2)}) collective-permute-start(f32[64,512]{1,0:T(8,128)} %convolution_add_fusion.7), channel_id=1, source_target_pairs={{0,4},{4,8},{8,12},{12,16},{16,20},{20,24},{24,28},{1,5},{5,9},{9,... | collective-permute-start | bytes 393224 | tf_op jit(solution)/shard_map/while/body/eval_jaxpr/ppermute | solution.py:89
  78.1 8.0 %collective-permute-start = (f32[64,512]{1,0:T(8,128)}, f32[64,512]{1,0:T(8,128)S(1)}, u32[]{:S(2)}, u32[]{:S(2)}) collective-permute-start(f32[64,512]{1,0:T(8,128)} %convolution_add_fusion.7), channel_id=1, source_target_pairs={{0,4},{4,8},{8,12},{12,16},{16,20},{20,24},{24,28},{1,5},{5,9},{9,... | collective-permute-start | bytes 393224 | tf_op jit(solution)/shard_map/while/body/eval_jaxpr/ppermute | solution.py:89
  90.1 8.0 %collective-permute-start = (f32[64,512]{1,0:T(8,128)}, f32[64,512]{1,0:T(8,128)S(1)}, u32[]{:S(2)}, u32[]{:S(2)}) collective-permute-start(f32[64,512]{1,0:T(8,128)} %convolution_add_fusion.7), channel_id=1, source_target_pairs={{0,4},{4,8},{8,12},{12,16},{16,20},{20,24},{24,28},{1,5},{5,9},{9,... | collective-permute-start | bytes 393224 | tf_op jit(solution)/shard_map/while/body/eval_jaxpr/ppermute | solution.py:89
  102.0 8.0 %collective-permute-start = (f32[64,512]{1,0:T(8,128)}, f32[64,512]{1,0:T(8,128)S(1)}, u32[]{:S(2)}, u32[]{:S(2)}) collective-permute-start(f32[64,512]{1,0:T(8,128)} %convolution_add_fusion.7), channel_id=1, source_target_pairs={{0,4},{4,8},{8,12},{12,16},{16,20},{20,24},{24,28},{1,5},{5,9},{9,... | collective-permute-start | bytes 393224 | tf_op jit(solution)/shard_map/while/body/eval_jaxpr/ppermute | solution.py:89
  109.9 0.6 copy-start.1
  120.1 8.4 %collective-permute-start.1 = (f32[64,512]{1,0:T(8,128)}, f32[64,512]{1,0:T(8,128)}, u32[]{:S(2)}, u32[]{:S(2)}) collective-permute-start(f32[64,512]{1,0:T(8,128)} %fusion.67), channel_id=1, source_target_pairs={{4,0},{8,4},{12,8},{16,12},{20,16},{24,20},{28,24},{5,1},{9,5},{13... | collective-permute-start | bytes 393224 | tf_op jit(solution)/shard_map/while/body/eval_jaxpr/ppermute | solution.py:103
  132.4 9.7 %collective-permute-start.1 = (f32[64,512]{1,0:T(8,128)}, f32[64,512]{1,0:T(8,128)}, u32[]{:S(2)}, u32[]{:S(2)}) collective-permute-start(f32[64,512]{1,0:T(8,128)} %fusion.67), channel_id=1, source_target_pairs={{4,0},{8,4},{12,8},{16,12},{20,16},{24,20},{28,24},{5,1},{9,5},{13... | collective-permute-start | bytes 393224 | tf_op jit(solution)/shard_map/while/body/eval_jaxpr/ppermute | solution.py:103
  145.9 9.0 %collective-permute-start.1 = (f32[64,512]{1,0:T(8,128)}, f32[64,512]{1,0:T(8,128)}, u32[]{:S(2)}, u32[]{:S(2)}) collective-permute-start(f32[64,512]{1,0:T(8,128)} %fusion.67), channel_id=1, source_target_pairs={{4,0},{8,4},{12,8},{16,12},{20,16},{24,20},{28,24},{5,1},{9,5},{13... | collective-permute-start | bytes 393224 | tf_op jit(solution)/shard_map/while/body/eval_jaxpr/ppermute | solution.py:103
  158.8 7.8 %collective-permute-start.1 = (f32[64,512]{1,0:T(8,128)}, f32[64,512]{1,0:T(8,128)}, u32[]{:S(2)}, u32[]{:S(2)}) collective-permute-start(f32[64,512]{1,0:T(8,128)} %fusion.67), channel_id=1, source_target_pairs={{4,0},{8,4},{12,8},{16,12},{20,16},{24,20},{28,24},{5,1},{9,5},{13... | collective-permute-start | bytes 393224 | tf_op jit(solution)/shard_map/while/body/eval_jaxpr/ppermute | solution.py:103
  170.5 8.1 %collective-permute-start.1 = (f32[64,512]{1,0:T(8,128)}, f32[64,512]{1,0:T(8,128)}, u32[]{:S(2)}, u32[]{:S(2)}) collective-permute-start(f32[64,512]{1,0:T(8,128)} %fusion.67), channel_id=1, source_target_pairs={{4,0},{8,4},{12,8},{16,12},{20,16},{24,20},{28,24},{5,1},{9,5},{13... | collective-permute-start | bytes 393224 | tf_op jit(solution)/shard_map/while/body/eval_jaxpr/ppermute | solution.py:103
  182.4 8.1 %collective-permute-start.1 = (f32[64,512]{1,0:T(8,128)}, f32[64,512]{1,0:T(8,128)}, u32[]{:S(2)}, u32[]{:S(2)}) collective-permute-start(f32[64,512]{1,0:T(8,128)} %fusion.67), channel_id=1, source_target_pairs={{4,0},{8,4},{12,8},{16,12},{20,16},{24,20},{28,24},{5,1},{9,5},{13... | collective-permute-start | bytes 393224 | tf_op jit(solution)/shard_map/while/body/eval_jaxpr/ppermute | solution.py:103
  194.4 8.1 %collective-permute-start.1 = (f32[64,512]{1,0:T(8,128)}, f32[64,512]{1,0:T(8,128)}, u32[]{:S(2)}, u32[]{:S(2)}) collective-permute-start(f32[64,512]{1,0:T(8,128)} %fusion.67), channel_id=1, source_target_pairs={{4,0},{8,4},{12,8},{16,12},{20,16},{24,20},{28,24},{5,1},{9,5},{13... | collective-permute-start | bytes 393224 | tf_op jit(solution)/shard_map/while/body/eval_jaxpr/ppermute | solution.py:103
